TPU v7x, 256 devices: a whole 4x4x8 slice. The times are simulated.
256 devices in a mesh: tm: 64 (over z, x, core), wafer: 4 (over y).
Axes of the slice: x: 4, y: 4, z: 8, core: 2. Of those that a mesh axis runs over, the one named last changes fastest.
Arguments:
- timestream: bfloat16 [1024, 262144], P('wafer', 'tm'), may hold values from -6 to 6
- sample_weight: bfloat16 [1024, 262144], P('wafer', 'tm'), may hold values from 0 to 4
- response: float32 [3, 1024], replicated, may hold values from -1 to 1
- band_filter: bfloat16 [256, 256], replicated, may hold values from -0.375 to 0.375
- whiten: bfloat16 [7, 1024, 1024], P(None, ('tm', 'wafer')), as said below
- group_wafer: int32 [64], replicated, may hold values from 0 to 6
- pointing: bfloat16 [1024, 6, 256, 256], P(('tm', 'wafer')), may hold values from -0.15625 to 0.15625
- tile_list: int32 [1024, 6], P(('tm', 'wafer')), may hold values from 0 to 2047, as said below
- tile_home: int32 [2048], replicated, may hold values from 0 to 2047, as said below
- solution: float32 [2048, 3, 256], P('tm'), may hold values from -6 to 6
- direction: float32 [2048, 3, 256], P('tm'), may hold values from -6 to 6
- cg_scalars: float32 [2], replicated, may hold values from 0.5 to 1.5
Outputs:
- solution_next: float32 [2048, 3, 256], P('tm')
- residual_next: float32 [2048, 3, 256], P('tm')
- direction_next: float32 [2048, 3, 256], P('tm')
Inputs may be any that keep to these rules, and one draw needn't show every extreme that they name: `tile_list`: the tiles named in the spans of one device (one index of tm and one of wafer) are all different; among them at most 2 have their row tile_home on one index of tm, and in every draw, for each index of wafer, some index of tm owns exactly 2 tiles named by every device of that wafer index. A permutation: row tile_home[i] of a map holds sky tile i. `whiten`: each whitening matrix is symmetric.
All inputs are finite; a program needn't handle non-finite values.
Results may differ from a plain program's by a relative error of at most 0.0033.
The roundings to bfloat16 on the way count: a program that leaves them out, or rounds other values in their place, can miss the bound.
Values may be sent and summed in bfloat16 or wider, within the bound.
No kernel may reach another device: no remote copies, remote signals or barrier semaphores. Data moves between devices by JAX's collectives and lax.ppermute only.
A program may use at most 128 MiB of HBM per device.

v0:
```python
import jax
import jax.numpy as jnp
from jax import lax
from jax.sharding import PartitionSpec as P


def shards(
    timestream,
    sample_weight,
    response,
    band_filter,
    whiten,
    group_wafer,
    pointing,
    tile_list,
    tile_home,
    solution,
    direction,
    cg_scalars,
):
    precise_mode = lax.Precision.HIGHEST
    tm_count = lax.axis_size("tm")
    tm_index = lax.axis_index("tm")
    step_size = cg_scalars[0]
    blend_weight = cg_scalars[1]
    updated = solution + step_size * direction
    short_map = updated.astype(jnp.bfloat16)
    tiles_own, comp_count, pixel_count = solution.shape
    spans_here, per_span = tile_list.shape
    samples = band_filter.shape[0]
    det_total = whiten.shape[2]
    row_count = spans_here * per_span
    capacity = max(2, (row_count + tm_count - 1) // tm_count)
    tile_ids = tile_list.reshape(row_count)
    home_rows = jnp.take(tile_home, tile_ids, axis=0)
    owners = home_rows // tiles_own
    local_slot = home_rows % tiles_own
    positions = jnp.arange(row_count, dtype=jnp.int32)
    earlier = (owners[:, None] == owners[None, :]) & (positions[None, :] < positions[:, None])
    before_count = jnp.sum(earlier.astype(jnp.int32), axis=1)
    targets = owners * capacity + before_count
    placing = targets[:, None] == jnp.arange(tm_count * capacity, dtype=jnp.int32)[None, :]
    requests = jnp.sum(jnp.where(placing, local_slot[:, None], 0), axis=0)
    requests = requests.reshape(tm_count, capacity)
    asked_slots = lax.all_to_all(requests, "tm", split_axis=0, concat_axis=0, tiled=True)
    served = jnp.take(short_map, asked_slots, axis=0)
    replies, asked_slots = (
        lax.all_to_all(served, "tm", split_axis=0, concat_axis=0, tiled=True),
        asked_slots,
    )
    fetched = jnp.take(
        replies.reshape(tm_count * capacity, comp_count, pixel_count), targets, axis=0
    )
    fetched = fetched.reshape(spans_here, per_span, comp_count, pixel_count)
    signal_parts = jnp.einsum(
        "cktp,ckjp->cjt", pointing, fetched, preferred_element_type=jnp.float32
    )
    wafer_pick = group_wafer[tm_index]
    matrix = lax.dynamic_index_in_dim(
        lax.all_gather(whiten, ("tm", "wafer"), axis=1, tiled=True), wafer_pick, 0, keepdims=False
    )
    columns, column_weights = (
        lax.all_to_all(timestream, "wafer", split_axis=1, concat_axis=0, tiled=True),
        lax.all_to_all(sample_weight, "wafer", split_axis=1, concat_axis=0, tiled=True),
    )
    column_weights = column_weights.astype(jnp.float32).reshape(det_total, spans_here, samples)
    signal = jnp.einsum("jd,cjt->dct", response, signal_parts, precision=precise_mode)
    errors = (
        (columns.astype(jnp.float32).reshape(det_total, spans_here, samples) - signal)
        * column_weights
    ).astype(jnp.bfloat16)
    filtered = jnp.dot(
        errors.reshape(det_total * spans_here, samples),
        band_filter,
        preferred_element_type=jnp.float32,
    )
    filtered = filtered.astype(jnp.bfloat16).reshape(det_total, spans_here * samples)
    whitened = jnp.dot(matrix, filtered, preferred_element_type=jnp.float32).astype(jnp.bfloat16)
    smoothed = lax.dot_general(
        whitened.reshape(det_total * spans_here, samples),
        band_filter,
        (((1,), (1,)), ((), ())),
        preferred_element_type=jnp.float32,
    )
    smoothed = smoothed.astype(jnp.bfloat16).reshape(det_total, spans_here, samples)
    stokes = jnp.einsum(
        "jd,dct->cjt",
        response,
        smoothed.astype(jnp.float32) * column_weights,
        precision=precise_mode,
    )
    stokes_short = stokes.astype(jnp.bfloat16)
    partial_value = jnp.einsum(
        "cjt,cktp->ckjp", stokes_short, pointing, preferred_element_type=jnp.float32
    )
    partial_value = partial_value.reshape(row_count, comp_count * pixel_count)
    outgoing = jnp.dot(placing.astype(jnp.float32).T, partial_value, precision=precise_mode)
    outgoing = outgoing.reshape(tm_count, capacity, comp_count, pixel_count)
    arrived = lax.all_to_all(outgoing, "tm", split_axis=0, concat_axis=0, tiled=True)
    slot_hits = (
        asked_slots.reshape(-1)[None, :] == jnp.arange(tiles_own, dtype=jnp.int32)[:, None]
    ).astype(jnp.float32)
    owned_sum = jnp.dot(
        slot_hits,
        arrived.reshape(tm_count * capacity, comp_count * pixel_count),
        precision=precise_mode,
    )
    owned_sum = owned_sum.reshape(tiles_own, comp_count, pixel_count)
    summed = lax.psum(owned_sum, "wafer")
    residual_next = summed * float(det_total) ** (-0.5)
    direction_next = residual_next + blend_weight * direction
    return (updated, residual_next, direction_next)


def solution(mesh):
    in_specs = (
        P("wafer", "tm"),
        P("wafer", "tm"),
        P(),
        P(),
        P(None, ("tm", "wafer"), None),
        P(),
        P(("tm", "wafer"), None, None, None),
        P(("tm", "wafer"), None),
        P(),
        P("tm", None, None),
        P("tm", None, None),
        P(),
    )
    out_specs = (P("tm", None, None), P("tm", None, None), P("tm", None, None))
    return jax.shard_map(shards, mesh=mesh, in_specs=in_specs, out_specs=out_specs, check_vma=False)
```

profile of v0, /device:TPU:2, one launch (start us, length us, event | category | flops | bytes accessed | tf_op | source)
XLA Modules:
  0.0 281.9 jit_solution(5731134282750877064)
XLA Ops:
  7.2 1.6 copy.111
  10.4 1.4 gather_fusion
  12.9 12.0 %all-to-all-start = ((s32[64,1,2]{2,1,0:T(1,128)}), s32[64,1,2]{2,1,0:T(1,128)S(1)}, u32[]{:S(2)}, u32[]{:S(2)}) async-start(s32[64,1,2]{2,1,0:T(1,128)} %bitcast.2), calls=%async_computation | async-start | bytes 65536 | tf_op jit(solution)/shard_map/all_to_all | solution.py:45
  24.9 1.4 fusion.34
  26.3 2.4 fusion.33
  28.7 4.8 %all-to-all-done = s32[64,1,2]{2,1,0:T(1,128)S(1)} async-done(((s32[64,1,2]{2,1,0:T(1,128)}), s32[64,1,2]{2,1,0:T(1,128)S(1)}, u32[]{:S(2)}, u32[]{:S(2)}) %all-to-all-start) | async-done | bytes 544 | tf_op jit(solution)/shard_map/all_to_all | solution.py:45
  34.1 0.8 gather_fusion.1
  34.9 0.9 broadcast_select_fusion
  35.9 5.5 %all-to-all-start.2 = ((bf16[64,2,3,256]{3,1,2,0:T(2,128)(2,1)}), bf16[64,2,3,256]{3,1,2,0:T(2,128)(2,1)S(1)}, u32[]{:S(2)}, u32[]{:S(2)}) async-start(bf16[64,2,3,256]{3,1,2,0:T(2,128)(2,1)} %broadcast_select_fusion), calls=%async_computation.2 | async-start | bytes 393216 | tf_op jit(solution)/shard_map/all_to_all | solution.py:48
  41.4 4.1 %copy.113 = bf16[256,4096]{0,1:T(8,128)(2,1)} copy(bf16[256,4096]{1,0:T(8,128)(2,1)} %param.12) | data formatting | bytes 4194304 | tf_op args[0]
  45.5 7.3 %all-to-all-done.2 = bf16[64,2,3,256]{3,1,2,0:T(2,128)(2,1)S(1)} async-done(((bf16[64,2,3,256]{3,1,2,0:T(2,128)(2,1)}), bf16[64,2,3,256]{3,1,2,0:T(2,128)(2,1)S(1)}, u32[]{:S(2)}, u32[]{:S(2)}) %all-to-all-start.2) | async-done | bytes 196640 | tf_op jit(solution)/shard_map/all_to_all | solution.py:48
  52.7 4.5 %all-to-all-start.1 = ((bf16[256,4,1024]{0,2,1:T(8,128)(2,1)}), bf16[256,4,1024]{0,2,1:T(8,128)(2,1)}, u32[]{:S(2)}, u32[]{:S(2)}) async-start(bf16[256,4,1024]{0,2,1:T(8,128)(2,1)} %bitcast.99), calls=%async_computation.1 | async-start | bytes 4194304 | tf_op jit(solution)/shard_map/all_to_all | solution.py:63
  57.2 4.1 %copy.123 = bf16[256,4096]{0,1:T(8,128)(2,1)} copy(bf16[256,4096]{1,0:T(8,128)(2,1)} %param.13) | data formatting | bytes 4194304 | tf_op args[1]
  61.3 25.7 %all-to-all-done.1 = bf16[256,4,1024]{0,2,1:T(8,128)(2,1)} async-done(((bf16[256,4,1024]{0,2,1:T(8,128)(2,1)}), bf16[256,4,1024]{0,2,1:T(8,128)(2,1)}, u32[]{:S(2)}, u32[]{:S(2)}) %all-to-all-start.1) | async-done | bytes 2097184 | tf_op jit(solution)/shard_map/all_to_all | solution.py:63
  87.1 4.6 %all-to-all-start.3 = ((bf16[256,4,1024]{0,2,1:T(8,128)(2,1)}), bf16[256,4,1024]{0,2,1:T(8,128)(2,1)}, u32[]{:S(2)}, u32[]{:S(2)}) async-start(bf16[256,4,1024]{0,2,1:T(8,128)(2,1)} %bitcast.98), calls=%async_computation.3 | async-start | bytes 4194304 | tf_op jit(solution)/shard_map/all_to_all | solution.py:64
  94.5 0.8 copy.120
  95.3 1.6 gather_fusion.2
  96.9 0.9 convolution_bitcast_fusion
  97.9 2.0 convert_bitcast_fusion.1
  99.8 4.8 %copy.114 = f32[4,256,1024]{1,0,2:T(4,128)} copy(f32[4,256,1024]{1,2,0:T(8,128)S(1)} %convert_bitcast_fusion.1) | data formatting | bytes 8388608 | tf_op jit(solution)/shard_map/convert_element_type | solution.py:69
  104.7 5.8 %reshape.326 = f32[1024,4,256]{0,2,1:T(8,128)} reshape(f32[4,256,1024]{1,0,2:T(4,128)} %copy.114) | data formatting | bytes 8388608 | tf_op jit(solution)/shard_map/convert_element_type | solution.py:69
  110.5 20.1 %all-to-all-done.3 = bf16[256,4,1024]{0,2,1:T(8,128)(2,1)} async-done(((bf16[256,4,1024]{0,2,1:T(8,128)(2,1)}), bf16[256,4,1024]{0,2,1:T(8,128)(2,1)}, u32[]{:S(2)}, u32[]{:S(2)}) %all-to-all-start.3) | async-done | bytes 2097184 | tf_op jit(solution)/shard_map/all_to_all | solution.py:64
  130.6 2.2 convert_bitcast_fusion
  132.8 4.7 %copy.124 = f32[4,256,1024]{1,0,2:T(4,128)} copy(f32[4,256,1024]{1,2,0:T(8,128)S(1)} %convert_bitcast_fusion) | data formatting | bytes 8388608 | tf_op jit(solution)/shard_map/convert_element_type | solution.py:66
  137.4 5.9 %reshape.327 = f32[1024,4,256]{0,2,1:T(8,128)} reshape(f32[4,256,1024]{1,0,2:T(4,128)} %copy.124) | data formatting | bytes 8388608 | tf_op jit(solution)/shard_map/convert_element_type | solution.py:66
  143.3 7.2 %fusion.2 = bf16[1024,4,256]{0,2,1:T(8,128)(2,1)} fusion(f32[1024,4,256]{0,2,1:T(8,128)} %reshape.327, f32[1024,4,256]{0,2,1:T(8,128)} %reshape.326, f32[4,3,256]{2,1,0:T(4,128)S(1)} %convolution_bitcast_fusion, f32[3,1024]{1,0:T(4,128)S(1)} %copy-done.4), kind=kOutput, calls=%fused_computation.8 | convolution fusion | flops 40894464 | bytes 10510336 | tf_op jit(solution)/shard_map/jd,cjt->dct/dot_general | solution.py:67
  150.5 4.3 %copy.125 = bf16[1024,4,256]{2,1,0:T(4,128)(2,1)} copy(bf16[1024,4,256]{0,2,1:T(8,128)(2,1)} %fusion.2) | data formatting | bytes 4194304 | tf_op jit(solution)/shard_map/convert_element_type | solution.py:71
  154.8 4.1 %reshape.321 = bf16[4096,256]{1,0:T(8,128)(2,1)} reshape(bf16[1024,4,256]{2,1,0:T(4,128)(2,1)} %copy.125) | data formatting | bytes 4194304 | tf_op jit(solution)/shard_map/reshape | solution.py:73
  158.9 3.7 %convolution_convert_fusion.1 = bf16[4096,256]{1,0:T(8,128)(2,1)} fusion(bf16[4096,256]{1,0:T(8,128)(2,1)} %reshape.321, bf16[256,256]{1,0:T(8,128)(2,1)S(1)} %copy-done.2), kind=kOutput, calls=%fused_computation.5 | convolution fusion | flops 537919488 | bytes 4325376 | tf_op jit(solution)/shard_map/dot_general | solution.py:72
  162.5 4.4 %reshape.322 = bf16[1024,1024]{1,0:T(8,128)(2,1)} reshape(bf16[4096,256]{1,0:T(8,128)(2,1)} %convolution_convert_fusion.1) | data formatting | bytes 4194304 | tf_op jit(solution)/shard_map/reshape | solution.py:77
  166.9 7.8 %constant_dynamic-slice_fusion = bf16[1,1024,1024]{2,0,1:T(2,128)(2,1)S(1)} fusion(bf16[7,1024,1024]{2,0,1:T(8,128)(2,1)} %all-gather.2.cloned.1.call-done, s32[]{:T(128)S(6)} %select_n.167), kind=kLoop, calls=%fused_computation.81 | loop fusion | bytes 4194308 | tf_op jit(solution)/shard_map/jit(dynamic_index_in_dim)/dynamic_slice | solution.py:59
  174.7 3.7 %fusion.6 = bf16[1024,1024]{1,0:T(8,128)(2,1)} fusion(bf16[1024,1024]{1,0:T(8,128)(2,1)S(1)} %copy-done.1, bf16[1,1024,1024]{2,0,1:T(2,128)(2,1)S(1)} %constant_dynamic-slice_fusion), kind=kOutput, calls=%fused_computation.15 | convolution fusion | flops 2148532224 | bytes 6291456 | tf_op jit(solution)/shard_map/dot_general | solution.py:78
  178.4 4.4 %reshape.323 = bf16[4096,256]{1,0:T(8,128)(2,1)} reshape(bf16[1024,1024]{1,0:T(8,128)(2,1)} %fusion.6) | data formatting | bytes 4194304 | tf_op jit(solution)/shard_map/reshape | solution.py:80
  182.8 4.3 %fusion = f32[4096,256]{1,0:T(8,128)} fusion(bf16[4096,256]{1,0:T(8,128)(2,1)} %reshape.323, bf16[256,256]{1,0:T(8,128)(2,1)S(1)} %copy-done.2), kind=kOutput, calls=%fused_computation.4 | convolution fusion | flops 538968064 | bytes 6422528 | tf_op jit(solution)/shard_map/dot_general | solution.py:79
  187.1 5.2 %reshape.328 = f32[1024,4,256]{2,1,0:T(4,128)} reshape(f32[4096,256]{1,0:T(8,128)} %fusion) | data formatting | bytes 8388608 | tf_op jit(solution)/shard_map/convert_element_type | solution.py:89
  192.3 5.2 %copy.126 = f32[1024,4,256]{0,2,1:T(8,128)} copy(f32[1024,4,256]{2,1,0:T(4,128)} %reshape.328) | data formatting | bytes 8388608 | tf_op jit(solution)/shard_map/convert_element_type | solution.py:89
  197.5 7.2 %fusion.10 = bf16[4,256,3,1]{1,2,3,0:T(4,128)(2,1)S(1)} fusion(f32[1024,4,256]{0,2,1:T(8,128)} %copy.126, f32[1024,4,256]{0,2,1:T(8,128)} %reshape.327, f32[3,1024]{1,0:T(4,128)S(1)} %copy-done.4), kind=kOutput, calls=%fused_computation.18 | convolution fusion | flops 38800384 | bytes 8407040 | tf_op jit(solution)/shard_map/jd,dct->cjt/dot_general | solution.py:86
  205.7 1.1 copy.129
  206.7 6.5 %all-to-all-start.4 = ((f32[64,2,3,256]{3,1,2,0:T(2,128)}), f32[64,2,3,256]{3,1,2,0:T(2,128)S(1)}, u32[]{:S(2)}, u32[]{:S(2)}) async-start(f32[64,2,3,256]{3,1,2,0:T(2,128)} %copy.129), calls=%async_computation.4 | async-start | bytes 786432 | tf_op jit(solution)/shard_map/all_to_all | solution.py:99
  213.8 2.1 reduce.3
  215.9 0.9 eq.71
  216.7 11.3 %all-to-all-done.4 = f32[64,2,3,256]{3,1,2,0:T(2,128)S(1)} async-done(((f32[64,2,3,256]{3,1,2,0:T(2,128)}), f32[64,2,3,256]{3,1,2,0:T(2,128)S(1)}, u32[]{:S(2)}, u32[]{:S(2)}) %all-to-all-start.4) | async-done | bytes 393248 | tf_op jit(solution)/shard_map/all_to_all | solution.py:99
  228.2 0.8 copy.141
  229.0 1.1 copy.131
  230.1 1.0 fusion.21
  231.1 1.6 copy.132
  232.7 40.0 %all-reduce.2.cloned.1.call-done = f32[32,3,256]{2,0,1:T(8,128)} async-done(((f32[32,3,256]{2,0,1:T(8,128)}), f32[32,3,256]{2,0,1:T(8,128)}) %all-reduce.2.cloned.1.call-update) | async-done | bytes 98320 | tf_op jit(solution)/shard_map/psum | solution.py:109
  272.7 2.3 multiply_add_fusion
  (47 shorter events, 5.8 us)
Async XLA Ops:
  7.2 89.8 %copy-start = (bf16[4,6,256,256]{3,2,1,0:T(8,128)(2,1)S(1)}, bf16[4,6,256,256]{3,2,1,0:T(8,128)(2,1)}, u32[]{:S(2)}) copy-start(bf16[4,6,256,256]{3,2,1,0:T(8,128)(2,1)} %param.18) | copy-start | bytes 9437188
  7.2 159.8 %all-gather.2.cloned.1.call-start = ((), (), s32[]{:S(2)}) async-start(), calls=%async_computation.5 | async-start | bytes 16842752 | tf_op jit(solution)/shard_map/all_gather | solution.py:60
  12.9 20.6 %all-to-all-start = ((s32[64,1,2]{2,1,0:T(1,128)}), s32[64,1,2]{2,1,0:T(1,128)S(1)}, u32[]{:S(2)}, u32[]{:S(2)}) async-start(s32[64,1,2]{2,1,0:T(1,128)} %bitcast.2), calls=%async_computation | async-start | bytes 65536 | tf_op jit(solution)/shard_map/all_to_all | solution.py:45
  33.5 0.6 copy-start.3
  35.9 16.9 %all-to-all-start.2 = ((bf16[64,2,3,256]{3,1,2,0:T(2,128)(2,1)}), bf16[64,2,3,256]{3,1,2,0:T(2,128)(2,1)S(1)}, u32[]{:S(2)}, u32[]{:S(2)}) async-start(bf16[64,2,3,256]{3,1,2,0:T(2,128)(2,1)} %broadcast_select_fusion), calls=%async_computation.2 | async-start | bytes 393216 | tf_op jit(solution)/shard_map/all_to_all | solution.py:48
  52.7 34.3 %all-to-all-start.1 = ((bf16[256,4,1024]{0,2,1:T(8,128)(2,1)}), bf16[256,4,1024]{0,2,1:T(8,128)(2,1)}, u32[]{:S(2)}, u32[]{:S(2)}) async-start(bf16[256,4,1024]{0,2,1:T(8,128)(2,1)} %bitcast.99), calls=%async_computation.1 | async-start | bytes 4194304 | tf_op jit(solution)/shard_map/all_to_all | solution.py:63
  61.3 30.6 %copy-start.6 = (s32[64]{0:T(128)S(1)}, s32[64]{0:T(128)}, u32[]{:S(2)}) copy-start(s32[64]{0:T(128)} %param.17) | copy-start | bytes 772
  61.3 33.1 %copy-start.5 = (s32[4,6]{1,0:T(4,128)S(1)}, s32[4,6]{1,0:T(4,128)}, u32[]{:S(2)}) copy-start(s32[4,6]{1,0:T(4,128)} %param.19) | copy-start | bytes 292
  87.1 43.5 %all-to-all-start.3 = ((bf16[256,4,1024]{0,2,1:T(8,128)(2,1)}), bf16[256,4,1024]{0,2,1:T(8,128)(2,1)}, u32[]{:S(2)}, u32[]{:S(2)}) async-start(bf16[256,4,1024]{0,2,1:T(8,128)(2,1)} %bitcast.98), calls=%async_computation.3 | async-start | bytes 4194304 | tf_op jit(solution)/shard_map/all_to_all | solution.py:64
  137.4 5.9 %copy-start.4 = (f32[3,1024]{1,0:T(4,128)S(1)}, f32[3,1024]{1,0:T(4,128)}, u32[]{:S(2)}) copy-start(f32[3,1024]{1,0:T(4,128)} %param.14) | copy-start | bytes 36868
  154.8 4.1 %copy-start.2 = (bf16[256,256]{1,0:T(8,128)(2,1)S(1)}, bf16[256,256]{1,0:T(8,128)(2,1)}, u32[]{:S(2)}) copy-start(bf16[256,256]{1,0:T(8,128)(2,1)} %param.15) | copy-start | bytes 393220
  166.9 7.8 %copy-start.1 = (bf16[1024,1024]{1,0:T(8,128)(2,1)S(1)}, bf16[1024,1024]{1,0:T(8,128)(2,1)}, u32[]{:S(2)}) copy-start(bf16[1024,1024]{1,0:T(8,128)(2,1)} %reshape.322) | copy-start | bytes 6291460
  206.7 21.3 %all-to-all-start.4 = ((f32[64,2,3,256]{3,1,2,0:T(2,128)}), f32[64,2,3,256]{3,1,2,0:T(2,128)S(1)}, u32[]{:S(2)}, u32[]{:S(2)}) async-start(f32[64,2,3,256]{3,1,2,0:T(2,128)} %copy.129), calls=%async_computation.4 | async-start | bytes 786432 | tf_op jit(solution)/shard_map/all_to_all | solution.py:99
  213.2 59.5 %all-reduce.2.cloned.1.call-start = ((), (), s32[]{:S(2)}) async-start(), calls=%async_computation.6 | async-start | bytes 196608 | tf_op jit(solution)/shard_map/psum | solution.py:109
Sparse Core Ops, SparseCore 0:
  12.2 136.2 all-gather.1
  231.3 41.4 all-reduce.1
where the time goes:
time: 284 us; the launch traced here: 282 us
  waiting for transfers between devices  109 us (38%)
  local copies, waits for them, and re-layouts  82.1 us (29%)
  starting transfers between devices  33.1 us (12%)
  matrix products  28.8 us (10%)
  between operations  16.2 us (6%)
  other arithmetic  12.3 us (4%)
    psum x1, waiting for transfers between devices, shards(): summed = lax.psum(owned_sum, 'wafer')  40 us
    all_to_all x1, waiting for transfers between devices, shards(): lax.all_to_all(timestream, 'wafer', split_axis=1, concat_axis=0, tiled=True)  25.7 us
    all_to_all x1, waiting for transfers between devices, shards(): lax.all_to_all(sample_weight, 'wafer', split_axis=1, concat_axis=0, tiled...  20.1 us
    unnamed x19, local copies, waits for them, and re-layouts  12.4 us
    all_to_all x1, starting transfers between devices, shards(): lax.all_to_all(requests, 'tm', split_axis=0, concat_axis=0, tiled=True)  12 us
    all_to_all x1, waiting for transfers between devices, shards(): lax.all_to_all(outgoing, 'tm', split_axis=0, concat_axis=0, tiled=True)  11.3 us
    convert_element_type x2, local copies, waits for them, and re-layouts, shards(): columns.astype(jnp.float32).reshape(det_total, spans_here, samples) - signal  10.7 us
    convert_element_type x2, local copies, waits for them, and re-layouts, shards(): column_weights.astype(jnp.float32).reshape(det_total, spans_here, samples)  10.6 us
  transfers between devices with their start and end apart: 7, of which 6 were waited for; matrix products, arithmetic and copies ran while one was open for 27% of the time, Pallas kernels for 0%

commit v1 on v0

--- a/solution.py
+++ b/solution.py
@@ -106,7 +106,9 @@
         precision=precise_mode,
     )
     owned_sum = owned_sum.reshape(tiles_own, comp_count, pixel_count)
-    summed = lax.psum(owned_sum, "wafer")
+    summed = owned_sum
+    for hop in (1, 2):
+        summed = summed + lax.ppermute(summed, "wafer", [(dev, dev ^ hop) for dev in range(4)])
     residual_next = summed * float(det_total) ** (-0.5)
     direction_next = residual_next + blend_weight * direction
     return (updated, residual_next, direction_next)

time: 284 us -> 252 us (0.89)
  waiting for transfers between devices: 109 us -> 76.9 us
    psum x1 -> x0, waiting for transfers between devices: 40 us -> none  [shards(): summed = lax.psum(owned_sum, 'wafer')]
    ppermute x0 -> x2, waiting for transfers between devices: none -> 7.72 us  [shards(): lax.ppermute(summed, 'wafer', [(dev, dev ^ hop) for dev in range(4)])]
  transfers between devices with their start and end apart: 7 -> 8, of which waited for: 6 -> 7; matrix products, arithmetic and copies ran while one was open for 27% -> 30% of each run, Pallas kernels for 0% -> 0%
where the time goes in v1:
time: 252 us; the launch traced here: 251 us
  local copies, waits for them, and re-layouts  82 us (33%)
  waiting for transfers between devices  76.9 us (31%)
  starting transfers between devices  35.2 us (14%)
  matrix products  28.2 us (11%)
  between operations  16.2 us (6%)
  other arithmetic  12.2 us (5%)
    all_to_all x1, waiting for transfers between devices, shards(): lax.all_to_all(timestream, 'wafer', split_axis=1, concat_axis=0, tiled=True)  25.7 us
    all_to_all x1, waiting for transfers between devices, shards(): lax.all_to_all(sample_weight, 'wafer', split_axis=1, concat_axis=0, tiled...  20 us
    unnamed x19, local copies, waits for them, and re-layouts  12.4 us
    all_to_all x1, starting transfers between devices, shards(): lax.all_to_all(requests, 'tm', split_axis=0, concat_axis=0, tiled=True)  12 us
    all_to_all x1, waiting for transfers between devices, shards(): lax.all_to_all(outgoing, 'tm', split_axis=0, concat_axis=0, tiled=True)  11.3 us
    convert_element_type x2, local copies, waits for them, and re-layouts, shards(): columns.astype(jnp.float32).reshape(det_total, spans_here, samples) - signal  10.7 us
    convert_element_type x2, local copies, waits for them, and re-layouts, shards(): column_weights.astype(jnp.float32).reshape(det_total, spans_here, samples)  10.6 us
    convert_element_type x2, local copies, waits for them, and re-layouts, shards(): smoothed.astype(jnp.float32) * column_weights  10.5 us
  transfers between devices with their start and end apart: 8, of which 7 were waited for; matrix products, arithmetic and copies ran while one was open for 30% of the time, Pallas kernels for 0%

profile of v1, /device:TPU:2, one launch (start us, length us, event | category | flops | bytes accessed | tf_op | source)
XLA Modules:
  0.0 250.6 jit_solution(5039228484432042915)
XLA Ops:
  7.2 1.6 copy.111
  10.4 1.4 gather_fusion
  12.9 12.0 %all-to-all-start = ((s32[64,1,2]{2,1,0:T(1,128)}), s32[64,1,2]{2,1,0:T(1,128)S(1)}, u32[]{:S(2)}, u32[]{:S(2)}) async-start(s32[64,1,2]{2,1,0:T(1,128)} %bitcast.2), calls=%async_computation | async-start | bytes 65536 | tf_op jit(solution)/shard_map/all_to_all | solution.py:45
  24.9 1.3 fusion.34
  26.2 2.4 fusion.33
  28.6 4.9 %all-to-all-done = s32[64,1,2]{2,1,0:T(1,128)S(1)} async-done(((s32[64,1,2]{2,1,0:T(1,128)}), s32[64,1,2]{2,1,0:T(1,128)S(1)}, u32[]{:S(2)}, u32[]{:S(2)}) %all-to-all-start) | async-done | bytes 544 | tf_op jit(solution)/shard_map/all_to_all | solution.py:45
  34.1 0.8 gather_fusion.1
  34.9 1.0 broadcast_select_fusion
  35.9 5.5 %all-to-all-start.2 = ((bf16[64,2,3,256]{3,1,2,0:T(2,128)(2,1)}), bf16[64,2,3,256]{3,1,2,0:T(2,128)(2,1)S(1)}, u32[]{:S(2)}, u32[]{:S(2)}) async-start(bf16[64,2,3,256]{3,1,2,0:T(2,128)(2,1)} %broadcast_select_fusion), calls=%async_computation.2 | async-start | bytes 393216 | tf_op jit(solution)/shard_map/all_to_all | solution.py:48
  41.4 4.1 %copy.113 = bf16[256,4096]{0,1:T(8,128)(2,1)} copy(bf16[256,4096]{1,0:T(8,128)(2,1)} %param.12) | data formatting | bytes 4194304 | tf_op args[0]
  45.5 7.2 %all-to-all-done.2 = bf16[64,2,3,256]{3,1,2,0:T(2,128)(2,1)S(1)} async-done(((bf16[64,2,3,256]{3,1,2,0:T(2,128)(2,1)}), bf16[64,2,3,256]{3,1,2,0:T(2,128)(2,1)S(1)}, u32[]{:S(2)}, u32[]{:S(2)}) %all-to-all-start.2) | async-done | bytes 196640 | tf_op jit(solution)/shard_map/all_to_all | solution.py:48
  52.7 4.6 %all-to-all-start.1 = ((bf16[256,4,1024]{0,2,1:T(8,128)(2,1)}), bf16[256,4,1024]{0,2,1:T(8,128)(2,1)}, u32[]{:S(2)}, u32[]{:S(2)}) async-start(bf16[256,4,1024]{0,2,1:T(8,128)(2,1)} %bitcast.99), calls=%async_computation.1 | async-start | bytes 4194304 | tf_op jit(solution)/shard_map/all_to_all | solution.py:63
  57.3 4.1 %copy.123 = bf16[256,4096]{0,1:T(8,128)(2,1)} copy(bf16[256,4096]{1,0:T(8,128)(2,1)} %param.13) | data formatting | bytes 4194304 | tf_op args[1]
  61.4 25.7 %all-to-all-done.1 = bf16[256,4,1024]{0,2,1:T(8,128)(2,1)} async-done(((bf16[256,4,1024]{0,2,1:T(8,128)(2,1)}), bf16[256,4,1024]{0,2,1:T(8,128)(2,1)}, u32[]{:S(2)}, u32[]{:S(2)}) %all-to-all-start.1) | async-done | bytes 2097184 | tf_op jit(solution)/shard_map/all_to_all | solution.py:63
  87.1 4.6 %all-to-all-start.3 = ((bf16[256,4,1024]{0,2,1:T(8,128)(2,1)}), bf16[256,4,1024]{0,2,1:T(8,128)(2,1)}, u32[]{:S(2)}, u32[]{:S(2)}) async-start(bf16[256,4,1024]{0,2,1:T(8,128)(2,1)} %bitcast.98), calls=%async_computation.3 | async-start | bytes 4194304 | tf_op jit(solution)/shard_map/all_to_all | solution.py:64
  95.3 1.6 gather_fusion.2
  97.0 0.9 convolution_bitcast_fusion
  97.9 2.0 convert_bitcast_fusion.1
  99.8 4.8 %copy.114 = f32[4,256,1024]{1,0,2:T(4,128)} copy(f32[4,256,1024]{1,2,0:T(8,128)S(1)} %convert_bitcast_fusion.1) | data formatting | bytes 8388608 | tf_op jit(solution)/shard_map/convert_element_type | solution.py:69
  104.7 5.8 %reshape.326 = f32[1024,4,256]{0,2,1:T(8,128)} reshape(f32[4,256,1024]{1,0,2:T(4,128)} %copy.114) | data formatting | bytes 8388608 | tf_op jit(solution)/shard_map/convert_element_type | solution.py:69
  110.5 20.0 %all-to-all-done.3 = bf16[256,4,1024]{0,2,1:T(8,128)(2,1)} async-done(((bf16[256,4,1024]{0,2,1:T(8,128)(2,1)}), bf16[256,4,1024]{0,2,1:T(8,128)(2,1)}, u32[]{:S(2)}, u32[]{:S(2)}) %all-to-all-start.3) | async-done | bytes 2097184 | tf_op jit(solution)/shard_map/all_to_all | solution.py:64
  130.5 2.2 convert_bitcast_fusion
  132.7 4.7 %copy.124 = f32[4,256,1024]{1,0,2:T(4,128)} copy(f32[4,256,1024]{1,2,0:T(8,128)S(1)} %convert_bitcast_fusion) | data formatting | bytes 8388608 | tf_op jit(solution)/shard_map/convert_element_type | solution.py:66
  137.4 5.9 %reshape.327 = f32[1024,4,256]{0,2,1:T(8,128)} reshape(f32[4,256,1024]{1,0,2:T(4,128)} %copy.124) | data formatting | bytes 8388608 | tf_op jit(solution)/shard_map/convert_element_type | solution.py:66
  143.3 7.2 %fusion.2 = bf16[1024,4,256]{0,2,1:T(8,128)(2,1)} fusion(f32[1024,4,256]{0,2,1:T(8,128)} %reshape.327, f32[1024,4,256]{0,2,1:T(8,128)} %reshape.326, f32[4,3,256]{2,1,0:T(4,128)S(1)} %convolution_bitcast_fusion, f32[3,1024]{1,0:T(4,128)S(1)} %copy-done.4), kind=kOutput, calls=%fused_computation.8 | convolution fusion | flops 40894464 | bytes 10510336 | tf_op jit(solution)/shard_map/jd,cjt->dct/dot_general | solution.py:67
  150.5 4.3 %copy.125 = bf16[1024,4,256]{2,1,0:T(4,128)(2,1)} copy(bf16[1024,4,256]{0,2,1:T(8,128)(2,1)} %fusion.2) | data formatting | bytes 4194304 | tf_op jit(solution)/shard_map/convert_element_type | solution.py:71
  154.8 4.0 %reshape.321 = bf16[4096,256]{1,0:T(8,128)(2,1)} reshape(bf16[1024,4,256]{2,1,0:T(4,128)(2,1)} %copy.125) | data formatting | bytes 4194304 | tf_op jit(solution)/shard_map/reshape | solution.py:73
  158.8 3.7 %convolution_convert_fusion.1 = bf16[4096,256]{1,0:T(8,128)(2,1)} fusion(bf16[4096,256]{1,0:T(8,128)(2,1)} %reshape.321, bf16[256,256]{1,0:T(8,128)(2,1)S(1)} %copy-done.2), kind=kOutput, calls=%fused_computation.5 | convolution fusion | flops 537919488 | bytes 4325376 | tf_op jit(solution)/shard_map/dot_general | solution.py:72
  162.5 4.4 %reshape.322 = bf16[1024,1024]{1,0:T(8,128)(2,1)} reshape(bf16[4096,256]{1,0:T(8,128)(2,1)} %convolution_convert_fusion.1) | data formatting | bytes 4194304 | tf_op jit(solution)/shard_map/reshape | solution.py:77
  166.8 7.8 %constant_dynamic-slice_fusion = bf16[1,1024,1024]{2,0,1:T(2,128)(2,1)S(1)} fusion(bf16[7,1024,1024]{2,0,1:T(8,128)(2,1)} %all-gather.2.cloned.1.call-done, s32[]{:T(128)S(6)} %select_n.167), kind=kLoop, calls=%fused_computation.81 | loop fusion | bytes 4194308 | tf_op jit(solution)/shard_map/jit(dynamic_index_in_dim)/dynamic_slice | solution.py:59
  174.6 3.7 %fusion.6 = bf16[1024,1024]{1,0:T(8,128)(2,1)} fusion(bf16[1024,1024]{1,0:T(8,128)(2,1)S(1)} %copy-done.1, bf16[1,1024,1024]{2,0,1:T(2,128)(2,1)S(1)} %constant_dynamic-slice_fusion), kind=kOutput, calls=%fused_computation.15 | convolution fusion | flops 2148532224 | bytes 6291456 | tf_op jit(solution)/shard_map/dot_general | solution.py:78
  178.3 4.4 %reshape.323 = bf16[4096,256]{1,0:T(8,128)(2,1)} reshape(bf16[1024,1024]{1,0:T(8,128)(2,1)} %fusion.6) | data formatting | bytes 4194304 | tf_op jit(solution)/shard_map/reshape | solution.py:80
  182.7 4.3 %fusion = f32[4096,256]{1,0:T(8,128)} fusion(bf16[4096,256]{1,0:T(8,128)(2,1)} %reshape.323, bf16[256,256]{1,0:T(8,128)(2,1)S(1)} %copy-done.2), kind=kOutput, calls=%fused_computation.4 | convolution fusion | flops 538968064 | bytes 6422528 | tf_op jit(solution)/shard_map/dot_general | solution.py:79
  187.0 5.2 %reshape.328 = f32[1024,4,256]{2,1,0:T(4,128)} reshape(f32[4096,256]{1,0:T(8,128)} %fusion) | data formatting | bytes 8388608 | tf_op jit(solution)/shard_map/convert_element_type | solution.py:89
  192.2 5.3 %copy.126 = f32[1024,4,256]{0,2,1:T(8,128)} copy(f32[1024,4,256]{2,1,0:T(4,128)} %reshape.328) | data formatting | bytes 8388608 | tf_op jit(solution)/shard_map/convert_element_type | solution.py:89
  197.4 7.2 %fusion.10 = bf16[4,256,3,1]{1,2,3,0:T(4,128)(2,1)S(1)} fusion(f32[1024,4,256]{0,2,1:T(8,128)} %copy.126, f32[1024,4,256]{0,2,1:T(8,128)} %reshape.327, f32[3,1024]{1,0:T(4,128)S(1)} %copy-done.4), kind=kOutput, calls=%fused_computation.18 | convolution fusion | flops 38800384 | bytes 8407040 | tf_op jit(solution)/shard_map/jd,dct->cjt/dot_general | solution.py:86
  205.6 1.1 copy.129
  206.6 6.6 %all-to-all-start.4 = ((f32[64,2,3,256]{3,1,2,0:T(2,128)}), f32[64,2,3,256]{3,1,2,0:T(2,128)S(1)}, u32[]{:S(2)}, u32[]{:S(2)}) async-start(f32[64,2,3,256]{3,1,2,0:T(2,128)} %copy.129), calls=%async_computation.4 | async-start | bytes 786432 | tf_op jit(solution)/shard_map/all_to_all | solution.py:99
  213.7 2.1 reduce.3
  215.8 0.9 eq.71
  216.7 11.3 %all-to-all-done.4 = f32[64,2,3,256]{3,1,2,0:T(2,128)S(1)} async-done(((f32[64,2,3,256]{3,1,2,0:T(2,128)}), f32[64,2,3,256]{3,1,2,0:T(2,128)S(1)}, u32[]{:S(2)}, u32[]{:S(2)}) %all-to-all-start.4) | async-done | bytes 393248 | tf_op jit(solution)/shard_map/all_to_all | solution.py:99
  228.2 0.8 copy.141
  229.0 1.1 copy.131
  231.2 4.2 %collective-permute-done = f32[32,3,256]{2,0,1:T(8,128)S(1)} collective-permute-done((f32[32,3,256]{2,0,1:T(8,128)S(1)}, f32[32,3,256]{2,0,1:T(8,128)S(1)}, u32[]{:S(2)}, u32[]{:S(2)}) %collective-permute-start) | collective-permute-done | bytes 98336 | tf_op jit(solution)/shard_map/ppermute | solution.py:111
  235.4 1.2 collective-permute-start.1
  236.6 1.6 copy.132
  238.2 3.5 %collective-permute-done.1 = f32[32,3,256]{2,0,1:T(8,128)S(1)} collective-permute-done((f32[32,3,256]{2,0,1:T(8,128)S(1)}, f32[32,3,256]{2,0,1:T(8,128)S(1)}, u32[]{:S(2)}, u32[]{:S(2)}) %collective-permute-start.1) | collective-permute-done | bytes 98336 | tf_op jit(solution)/shard_map/ppermute | solution.py:111
  241.6 2.1 multiply_add_fusion
  (49 shorter events, 7.6 us)
Async XLA Ops:
  7.2 89.8 %copy-start = (bf16[4,6,256,256]{3,2,1,0:T(8,128)(2,1)S(1)}, bf16[4,6,256,256]{3,2,1,0:T(8,128)(2,1)}, u32[]{:S(2)}) copy-start(bf16[4,6,256,256]{3,2,1,0:T(8,128)(2,1)} %param.18) | copy-start | bytes 9437188
  7.2 159.7 %all-gather.2.cloned.1.call-start = ((), (), s32[]{:S(2)}) async-start(), calls=%async_computation.5 | async-start | bytes 16842752 | tf_op jit(solution)/shard_map/all_gather | solution.py:60
  12.9 20.6 %all-to-all-start = ((s32[64,1,2]{2,1,0:T(1,128)}), s32[64,1,2]{2,1,0:T(1,128)S(1)}, u32[]{:S(2)}, u32[]{:S(2)}) async-start(s32[64,1,2]{2,1,0:T(1,128)} %bitcast.2), calls=%async_computation | async-start | bytes 65536 | tf_op jit(solution)/shard_map/all_to_all | solution.py:45
  33.5 0.6 copy-start.3
  35.9 16.8 %all-to-all-start.2 = ((bf16[64,2,3,256]{3,1,2,0:T(2,128)(2,1)}), bf16[64,2,3,256]{3,1,2,0:T(2,128)(2,1)S(1)}, u32[]{:S(2)}, u32[]{:S(2)}) async-start(bf16[64,2,3,256]{3,1,2,0:T(2,128)(2,1)} %broadcast_select_fusion), calls=%async_computation.2 | async-start | bytes 393216 | tf_op jit(solution)/shard_map/all_to_all | solution.py:48
  52.7 34.4 %all-to-all-start.1 = ((bf16[256,4,1024]{0,2,1:T(8,128)(2,1)}), bf16[256,4,1024]{0,2,1:T(8,128)(2,1)}, u32[]{:S(2)}, u32[]{:S(2)}) async-start(bf16[256,4,1024]{0,2,1:T(8,128)(2,1)} %bitcast.99), calls=%async_computation.1 | async-start | bytes 4194304 | tf_op jit(solution)/shard_map/all_to_all | solution.py:63
  61.4 30.5 %copy-start.6 = (s32[64]{0:T(128)S(1)}, s32[64]{0:T(128)}, u32[]{:S(2)}) copy-start(s32[64]{0:T(128)} %param.17) | copy-start | bytes 772
  61.4 33.1 %copy-start.5 = (s32[4,6]{1,0:T(4,128)S(1)}, s32[4,6]{1,0:T(4,128)}, u32[]{:S(2)}) copy-start(s32[4,6]{1,0:T(4,128)} %param.19) | copy-start | bytes 292
  87.1 43.4 %all-to-all-start.3 = ((bf16[256,4,1024]{0,2,1:T(8,128)(2,1)}), bf16[256,4,1024]{0,2,1:T(8,128)(2,1)}, u32[]{:S(2)}, u32[]{:S(2)}) async-start(bf16[256,4,1024]{0,2,1:T(8,128)(2,1)} %bitcast.98), calls=%async_computation.3 | async-start | bytes 4194304 | tf_op jit(solution)/shard_map/all_to_all | solution.py:64
  137.4 5.9 %copy-start.4 = (f32[3,1024]{1,0:T(4,128)S(1)}, f32[3,1024]{1,0:T(4,128)}, u32[]{:S(2)}) copy-start(f32[3,1024]{1,0:T(4,128)} %param.14) | copy-start | bytes 36868
  154.8 4.0 %copy-start.2 = (bf16[256,256]{1,0:T(8,128)(2,1)S(1)}, bf16[256,256]{1,0:T(8,128)(2,1)}, u32[]{:S(2)}) copy-start(bf16[256,256]{1,0:T(8,128)(2,1)} %param.15) | copy-start | bytes 393220
  166.8 7.8 %copy-start.1 = (bf16[1024,1024]{1,0:T(8,128)(2,1)S(1)}, bf16[1024,1024]{1,0:T(8,128)(2,1)}, u32[]{:S(2)}) copy-start(bf16[1024,1024]{1,0:T(8,128)(2,1)} %reshape.322) | copy-start | bytes 6291460
  206.6 21.4 %all-to-all-start.4 = ((f32[64,2,3,256]{3,1,2,0:T(2,128)}), f32[64,2,3,256]{3,1,2,0:T(2,128)S(1)}, u32[]{:S(2)}, u32[]{:S(2)}) async-start(f32[64,2,3,256]{3,1,2,0:T(2,128)} %copy.129), calls=%async_computation.4 | async-start | bytes 786432 | tf_op jit(solution)/shard_map/all_to_all | solution.py:99
  230.5 4.9 %collective-permute-start = (f32[32,3,256]{2,0,1:T(8,128)S(1)}, f32[32,3,256]{2,0,1:T(8,128)S(1)}, u32[]{:S(2)}, u32[]{:S(2)}) collective-permute-start(f32[32,3,256]{2,0,1:T(8,128)S(1)} %fusion.21), channel_id=1, source_target_pairs={{0,1},{1,0},{2,3},{3,2},{4,5},{5,4},{6,7},{7,6},{8,9},{9,8},{10,11... | collective-permute-start | bytes 294920 | tf_op jit(solution)/shard_map/ppermute | solution.py:111
  235.4 6.2 %collective-permute-start.1 = (f32[32,3,256]{2,0,1:T(8,128)S(1)}, f32[32,3,256]{2,0,1:T(8,128)S(1)}, u32[]{:S(2)}, u32[]{:S(2)}) collective-permute-start(f32[32,3,256]{2,0,1:T(8,128)S(1)} %add.164), channel_id=1, source_target_pairs={{0,2},{1,3},{2,0},{3,1},{4,6},{5,7},{6,4},{7,5},{8,10},{9,11},{10,... | collective-permute-start | bytes 294920 | tf_op jit(solution)/shard_map/ppermute | solution.py:111
Sparse Core Ops, SparseCore 0:
  12.2 136.2 all-gather.1
